TPU v7x, 128 devices: a whole 4x4x4 slice. The times are simulated.
128 devices in a mesh: sector: 8 (over y, core), row: 16 (over x, z).
Axes of the slice: x: 4, y: 4, z: 4, core: 2. Of those that a mesh axis runs over, the one named last changes fastest.
Arguments:
- amplitudes: bfloat16 [8192, 4, 8192], P('sector', None, 'row'), may hold values from -6 to 6
- next_site: bfloat16 [8, 4, 8192, 2048], P('sector', None, 'row'), may hold values from -0.03125 to 0.03125
- sector_rows: int32 [8], replicated, may hold values from 512 to 1024, as said below
- moves: int32 [2, 8], replicated, may hold values from 0 to 128, as said below
- angles: float32 [2, 8, 128], replicated, may hold values from -3.140625 to 3.140625
- ranks: int32 [8], replicated, may hold values from 256 to 1024, as said below
Outputs:
- canonical: bfloat16 [2048, 8192], P('row', 'sector')
Inputs may be any that keep to these rules, and one draw needn't show every extreme that they name: `sector_rows`: one sector has exactly 1024 live rows and another exactly 512. `moves`: the entry of the last sector is 0, every other entry is 1 or more; for each gate some pair moves exactly 128 rows. `ranks`: each sector keeps at least half of its live rows and at most all of them; one sector keeps 1024 rows and one keeps 1024 // 4.
All inputs are finite; a program needn't handle non-finite values.
Results may differ from a plain program's by a relative error of at most 0.014.
Values may be sent and summed in bfloat16 or wider, within the bound.
No kernel may reach another device: no remote copies, remote signals or barrier semaphores. Data moves between devices by JAX's collectives and lax.ppermute only.
A program may use at most 128 MiB of HBM per device.

v0:
```python
import math
import jax
import jax.numpy as jnp
from jax import lax
from jax.sharding import PartitionSpec as P

KOUT = 2048
BLOCK = 128
HI = lax.Precision.HIGHEST


def shifted(x, axis, by):
    size = lax.axis_size(axis)
    pairs = [(i, i + by) for i in range(size) if 0 <= i + by < size]
    return lax.ppermute(x, axis, pairs)


def rotated_window(own, partner, angle, count, sign):
    slot_index = jnp.arange(own.shape[0])
    own32 = own.astype(jnp.float32)
    partner32 = partner.astype(jnp.float32)
    cos_t = jnp.cos(angle)[:, None, None]
    sin_t = jnp.sin(angle)[:, None, None]
    if sign < 0:
        new = cos_t * own32 - sin_t * partner32
    else:
        new = sin_t * partner32 + cos_t * own32
    return jnp.where((slot_index < count)[:, None, None], new, own32).astype(jnp.bfloat16)


def dot(a, b):
    return jnp.dot(a, b, precision=HI, preferred_element_type=jnp.float32)


def cholesky_solve(gram, rhs):
    n = gram.shape[0]
    eye = jnp.eye(BLOCK, dtype=jnp.float32)
    trailing = gram
    rest = rhs
    solved = []
    for start in range(0, n, BLOCK):
        diag = trailing[:BLOCK, :BLOCK]
        factor = jnp.linalg.cholesky(diag)
        inverse = lax.linalg.triangular_solve(factor, eye, left_side=True, lower=True)
        head = dot(inverse, rest[:BLOCK])
        solved.append(head)
        if start + BLOCK < n:
            panel = lax.dot_general(
                trailing[BLOCK:, :BLOCK],
                inverse,
                (((1,), (1,)), ((), ())),
                precision=HI,
                preferred_element_type=jnp.float32,
            )
            trailing = trailing[BLOCK:, BLOCK:] - lax.dot_general(
                panel,
                panel,
                (((1,), (1,)), ((), ())),
                precision=HI,
                preferred_element_type=jnp.float32,
            )
            rest = rest[BLOCK:] - dot(panel, head)
    return jnp.concatenate(solved, 0)


def per_device(amplitudes, next_site, sector_rows, moves, angles, ranks):
    sector_id = lax.axis_index("sector")
    rows = amplitudes.shape[0]
    move_rows = angles.shape[-1]
    row_index = jnp.arange(rows)
    live_rows = sector_rows[sector_id]
    prev_id = jnp.maximum(sector_id - 1, 0)
    count_here = moves[:, sector_id]
    count_prev = jnp.where(sector_id > 0, moves[:, prev_id], 0)
    masked = jnp.where(
        (row_index < live_rows)[:, None, None], amplitudes, jnp.zeros((), amplitudes.dtype)
    )
    padded = jnp.concatenate([masked, jnp.zeros((move_rows,) + masked.shape[1:], masked.dtype)], 0)
    starts_a = [live_rows - count_here[0], live_rows - count_here[0] - count_here[1]]
    starts_b = [jnp.int32(0), count_prev[0]]
    own_a = [lax.dynamic_slice_in_dim(padded, s, move_rows, 0) for s in starts_a]
    own_b = [lax.dynamic_slice_in_dim(padded, s, move_rows, 0) for s in starts_b]
    from_below = [shifted(w, "sector", 1) for w in own_a]
    from_above = [shifted(w, "sector", -1) for w in own_b]
    new_a = [
        rotated_window(own_a[g], from_above[g], angles[g][sector_id], count_here[g], -1)
        for g in range(2)
    ]
    new_b = [
        rotated_window(own_b[g], from_below[g], angles[g][prev_id], count_prev[g], 1)
        for g in range(2)
    ]
    padded = lax.dynamic_update_slice_in_dim(padded, new_a[1], starts_a[1], 0)
    padded = lax.dynamic_update_slice_in_dim(padded, new_a[0], starts_a[0], 0)
    padded = lax.dynamic_update_slice_in_dim(padded, new_b[0], starts_b[0], 0)
    padded = lax.dynamic_update_slice_in_dim(padded, new_b[1], starts_b[1], 0)
    block_rows = padded[:rows]
    site_tensor = next_site[0]
    contracted = lax.psum_scatter(
        jnp.einsum("prk,lpr->kl", site_tensor, block_rows, preferred_element_type=jnp.float32),
        "row",
        scatter_dimension=0,
        tiled=True,
    ).astype(jnp.bfloat16)
    gathered = lax.all_gather(contracted, "row", axis=0, tiled=True)
    gram_matrix = lax.dot_general(
        gathered, gathered, (((0,), (0,)), ((), ())), preferred_element_type=jnp.float32
    )
    dead_rows = (row_index >= live_rows).astype(jnp.float32)
    gram_matrix = gram_matrix + jnp.diag(dead_rows)
    solved = cholesky_solve(gram_matrix, contracted.astype(jnp.float32).T).T
    kept_mask = ((row_index >= live_rows - ranks[sector_id]) & (row_index < live_rows)).astype(
        jnp.float32
    )
    return (solved * math.sqrt(KOUT) * kept_mask[None, :]).astype(jnp.bfloat16)


def solution(mesh):
    placed = (P("sector", None, "row"), P("sector", None, "row", None), P(), P(), P(), P())
    return jax.shard_map(
        per_device, mesh=mesh, in_specs=placed, out_specs=P("row", "sector"), check_vma=False
    )
```

profile of v0, /device:TPU:0, one launch (start us, length us, event | category | flops | bytes accessed | tf_op | source)
XLA Modules:
  0.0 469.1 jit_solution(3784771538041529058)
XLA Ops:
  6.5 1.3 dynamic_slice.36
  11.8 5.1 %copy_select_fusion = bf16[1024,4,512]{2,0,1:T(8,128)(2,1)S(1)} fusion(bf16[1024,4,512]{2,1,0:T(4,128)(2,1)} %param.9, pred[1024]{0:T(1024)(128)(4,1)S(1)} %iota_compare_fusion.13), kind=kLoop, calls=%fused_computation.4 | loop fusion | flops 2097152 | bytes 8389632 | tf_op jit(solution)/shard_map/jit(_where)/select_n | solution.py:75
  16.9 1.9 copy-done
  19.0 1.3 collective-permute-start.1
  20.3 3.1 collective-permute-start.3
  27.2 2.0 fusion.9
  29.1 1.3 collective-permute-start
  30.4 6.1 %collective-permute-start.2 = (bf16[128,4,512]{2,0,1:T(8,128)(2,1)S(1)}, bf16[128,4,512]{2,0,1:T(8,128)(2,1)S(1)}, u32[]{:S(2)}, u32[]{:S(2)}) collective-permute-start(bf16[128,4,512]{2,0,1:T(8,128)(2,1)S(1)} %get-tuple-element.10), channel_id=1, source_target_pairs={{0,16},{16,32},{32,48},{48,64},{64,80},{80,96},{96,112},{1,17},{17... | collective-permute-start | bytes 1572872 | tf_op jit(solution)/shard_map/ppermute | solution.py:15
  36.6 2.5 concatenate.6
  40.7 5.6 %dynamic_update_slice.12 = bf16[1152,4,512]{2,0,1:T(8,128)(2,1)} dynamic-update-slice(bf16[1152,4,512]{2,0,1:T(8,128)(2,1)} %concatenate.6, bf16[128,4,512]{2,0,1:T(8,128)(2,1)S(1)} %fusion.7, s32[]{:T(128)S(6)} %select_n.58, s32[]{:T(128)} %constant.51.clone.1, s32[]{:T(128)} %constant.51.clone.1) | dynamic-update-slice | bytes 1048580 | tf_op jit(solution)/shard_map/dynamic_update_slice | solution.py:93
  46.2 5.6 %dynamic_update_slice.13 = bf16[1152,4,512]{2,0,1:T(8,128)(2,1)} dynamic-update-slice(bf16[1152,4,512]{2,0,1:T(8,128)(2,1)} %dynamic_update_slice.12, bf16[128,4,512]{2,0,1:T(8,128)(2,1)S(1)} %get-tuple-element.9, s32[]{:T(128)S(6)} %select_n.63, s32[]{:T(128)} %constant.51.clone.1, s32[]{:T(128)} %constant.51.clone.1) | dynamic-update-slice | bytes 1048580 | tf_op jit(solution)/shard_map/dynamic_update_slice | solution.py:94
  51.8 2.2 fusion.14
  54.0 5.5 %dynamic_update_slice.15 = bf16[1152,4,512]{2,0,1:T(8,128)(2,1)} dynamic-update-slice(bf16[1152,4,512]{2,0,1:T(8,128)(2,1)} %fusion.14, bf16[128,4,512]{2,0,1:T(8,128)(2,1)S(1)} %get-tuple-element.11, s32[]{:T(128)S(6)} %select_n.61, s32[]{:T(128)} %constant.51.clone.1, s32[]{:T(128)} %constant.51.clone.1) | dynamic-update-slice | bytes 1048580 | tf_op jit(solution)/shard_map/dynamic_update_slice | solution.py:96
  59.5 14.4 %fusion.2 = f32[2048,1024]{0,1:T(8,128)} fusion(bf16[1,4,512,2048]{3,2,1,0:T(8,128)(2,1)} %param.10, bf16[1152,4,512]{2,0,1:T(8,128)(2,1)} %dynamic_update_slice.15), kind=kOutput, calls=%fused_computation.2 | convolution fusion | flops 8589934592 | bytes 20971520 | tf_op jit(solution)/shard_map/prk,lpr->kl/dot_general | solution.py:100
  74.0 90.8 %reduce-scatter.2.cloned.1.call-done = f32[128,1024]{0,1:T(8,128)} async-done(((f32[2048,1024]{0,1:T(8,128)}), f32[128,1024]{0,1:T(8,128)}) %reduce-scatter.2.cloned.1.call-update) | async-done | bytes 524304 | tf_op jit(solution)/shard_map/reduce_scatter | solution.py:99
  164.9 1.8 convert_element_type.87
  169.7 1.1 convert_bitcast_fusion
  170.8 53.2 %all-gather.2.cloned.1.call-done = bf16[2048,1024]{0,1:T(8,128)(2,1)} async-done(((bf16[128,1024]{0,1:T(8,128)(2,1)}), bf16[2048,1024]{0,1:T(8,128)(2,1)}) %all-gather.2.cloned.1.call-update) | async-done | bytes 4194320 | tf_op jit(solution)/shard_map/all_gather | solution.py:105
  224.0 8.6 %select_add_fusion = f32[1024,1024]{0,1:T(8,128)S(1)} fusion(f32[1024]{0:T(1024)S(1)} %fusion.84, bf16[2048,1024]{0,1:T(8,128)(2,1)} %all-gather.2.cloned.1.call-done), kind=kOutput, calls=%fused_computation.5 | convolution fusion | flops 4298113024 | bytes 8392704 | tf_op jit(solution)/shard_map/dot_general | solution.py:106
  232.6 1.9 copy-done.8
  235.5 11.7 %cholesky.134 = f32[128,128]{1,0:T(8,128)S(1)} custom-call(f32[128,128]{1,0:T(8,128)S(1)} %fusion.81), custom_call_target="Cholesky" | custom-call | tf_op jit(solution)/shard_map/jit(cholesky)/cholesky | solution.py:43
  248.6 9.8 %custom-call.12 = f32[1,128,128]{1,2,0:T(8,128)S(1)} custom-call(f32[1,128,128]{2,1,0:T(8,128)S(1)} %fusion.44), custom_call_target="InvertDiagBlocksLowerTriangular" | custom-call | tf_op jit(solution)/shard_map/triangular_solve/custom-call.0 | solution.py:44
  259.3 1.9 fusion.15
  262.0 4.6 slice_subtract_fusion
  268.8 12.7 %cholesky.145 = f32[128,128]{1,0:T(8,128)S(1)} custom-call(f32[128,128]{1,0:T(8,128)} %fusion.79), custom_call_target="Cholesky" | custom-call | tf_op jit(solution)/shard_map/jit(cholesky)/cholesky | solution.py:43
  282.2 1.2 fusion.45
  283.4 10.6 %custom-call.13 = f32[1,128,128]{1,2,0:T(8,128)S(1)} custom-call(f32[1,128,128]{2,1,0:T(8,128)} %fusion.45), custom_call_target="InvertDiagBlocksLowerTriangular" | custom-call | tf_op jit(solution)/shard_map/triangular_solve/custom-call.0 | solution.py:44
  295.8 2.0 slice_subtract_fusion.1
  297.9 1.4 copy-done.2
  300.2 11.7 %cholesky.156 = f32[128,128]{1,0:T(8,128)S(1)} custom-call(f32[128,128]{1,0:T(8,128)S(1)} %fusion.77), custom_call_target="Cholesky" | custom-call | tf_op jit(solution)/shard_map/jit(cholesky)/cholesky | solution.py:43
  313.3 10.0 %custom-call.14 = f32[1,128,128]{1,2,0:T(8,128)S(1)} custom-call(f32[1,128,128]{2,1,0:T(8,128)S(1)} %fusion.46), custom_call_target="InvertDiagBlocksLowerTriangular" | custom-call | tf_op jit(solution)/shard_map/triangular_solve/custom-call.0 | solution.py:44
  323.6 1.7 fusion.19
  325.3 2.9 slice_subtract_fusion.2
  328.3 11.7 %cholesky.167 = f32[128,128]{1,0:T(8,128)S(1)} custom-call(f32[128,128]{1,0:T(8,128)S(1)} %fusion.75), custom_call_target="Cholesky" | custom-call | tf_op jit(solution)/shard_map/jit(cholesky)/cholesky | solution.py:43
  341.5 9.8 %custom-call.15 = f32[1,128,128]{1,2,0:T(8,128)S(1)} custom-call(f32[1,128,128]{2,1,0:T(8,128)S(1)} %fusion.47), custom_call_target="InvertDiagBlocksLowerTriangular" | custom-call | tf_op jit(solution)/shard_map/triangular_solve/custom-call.0 | solution.py:44
  352.2 1.0 convolution_subtract_fusion
  355.2 12.1 %cholesky.178 = f32[128,128]{1,0:T(8,128)S(1)} custom-call(f32[128,128]{1,0:T(8,128)S(1)} %fusion.73), custom_call_target="Cholesky" | custom-call | tf_op jit(solution)/shard_map/jit(cholesky)/cholesky | solution.py:43
  368.8 9.8 %custom-call.16 = f32[1,128,128]{1,2,0:T(8,128)S(1)} custom-call(f32[1,128,128]{2,1,0:T(8,128)S(1)} %fusion.48), custom_call_target="InvertDiagBlocksLowerTriangular" | custom-call | tf_op jit(solution)/shard_map/triangular_solve/custom-call.0 | solution.py:44
  378.9 1.4 fusion.40
  380.3 1.7 convolution_subtract_fusion.1
  382.1 11.7 %cholesky.189 = f32[128,128]{1,0:T(8,128)S(1)} custom-call(f32[128,128]{1,0:T(8,128)S(1)} %fusion.71), custom_call_target="Cholesky" | custom-call | tf_op jit(solution)/shard_map/jit(cholesky)/cholesky | solution.py:43
  395.3 9.8 %custom-call.17 = f32[1,128,128]{1,2,0:T(8,128)S(1)} custom-call(f32[1,128,128]{2,1,0:T(8,128)S(1)} %fusion.49), custom_call_target="InvertDiagBlocksLowerTriangular" | custom-call | tf_op jit(solution)/shard_map/triangular_solve/custom-call.0 | solution.py:44
  407.1 11.7 %cholesky.200 = f32[128,128]{1,0:T(8,128)S(1)} custom-call(f32[128,128]{1,0:T(8,128)S(1)} %fusion.69), custom_call_target="Cholesky" | custom-call | tf_op jit(solution)/shard_map/jit(cholesky)/cholesky | solution.py:43
  420.0 9.8 %custom-call.18 = f32[1,128,128]{1,2,0:T(8,128)S(1)} custom-call(f32[1,128,128]{2,1,0:T(8,128)S(1)} %fusion.50), custom_call_target="InvertDiagBlocksLowerTriangular" | custom-call | tf_op jit(solution)/shard_map/triangular_solve/custom-call.0 | solution.py:44
  432.0 1.0 constant_dynamic-update-slice_fusion.5
  433.5 1.0 constant_dynamic-update-slice_fusion.4
  437.4 11.9 %cholesky.211 = f32[128,128]{1,0:T(8,128)S(1)} custom-call(f32[128,128]{1,0:T(8,128)S(1)} %fusion.67), custom_call_target="Cholesky" | custom-call | tf_op jit(solution)/shard_map/jit(cholesky)/cholesky | solution.py:43
  450.7 9.8 %custom-call.19 = f32[1,128,128]{1,2,0:T(8,128)S(1)} custom-call(f32[1,128,128]{2,1,0:T(8,128)S(1)} %fusion.51), custom_call_target="InvertDiagBlocksLowerTriangular" | custom-call | tf_op jit(solution)/shard_map/triangular_solve/custom-call.0 | solution.py:44
  (126 shorter events, 37.6 us)
Async XLA Ops:
  6.5 158.3 %reduce-scatter.2.cloned.1.call-start = ((), (), s32[]{:S(2)}) async-start(), calls=%async_computation.1 | async-start | bytes 8912896 | tf_op jit(solution)/shard_map/reduce_scatter | solution.py:99
  16.9 1.9 copy-start
  18.8 8.2 %copy-start.14 = (f32[2,8,128]{2,1,0:T(8,128)S(1)}, f32[2,8,128]{2,1,0:T(8,128)}, u32[]{:S(2)}) copy-start(f32[2,8,128]{2,1,0:T(8,128)} %param.13) | copy-start | bytes 24580
  19.0 8.1 %collective-permute-start.1 = (bf16[128,4,512]{2,0,1:T(8,128)(2,1)S(1)}, bf16[128,4,512]{2,0,1:T(8,128)(2,1)S(1)}, u32[]{:S(2)}, u32[]{:S(2)}) collective-permute-start(bf16[128,4,512]{2,0,1:T(8,128)(2,1)S(1)} %get-tuple-element.13), channel_id=1, source_target_pairs={{16,0},{32,16},{48,32},{64,48},{80,64},{96,80},{112,96},{17,1},{33... | collective-permute-start | bytes 1572872 | tf_op jit(solution)/shard_map/ppermute | solution.py:15
  20.3 6.8 %collective-permute-start.3 = (bf16[128,4,512]{2,0,1:T(8,128)(2,1)S(1)}, bf16[128,4,512]{2,0,1:T(8,128)(2,1)S(1)}, u32[]{:S(2)}, u32[]{:S(2)}) collective-permute-start(bf16[128,4,512]{2,0,1:T(8,128)(2,1)S(1)} %get-tuple-element.14), channel_id=1, source_target_pairs={{0,16},{16,32},{32,48},{48,64},{64,80},{80,96},{96,112},{1,17},{17... | collective-permute-start | bytes 1572872 | tf_op jit(solution)/shard_map/ppermute | solution.py:15
  25.4 11.2 %copy-start.1 = (bf16[1024,4,512]{2,0,1:T(8,128)(2,1)S(1)}, bf16[1024,4,512]{2,0,1:T(8,128)(2,1)}, u32[]{:S(2)}) copy-start(bf16[1024,4,512]{2,0,1:T(8,128)(2,1)} %copy-done) | copy-start | bytes 12582916
  29.1 11.2 %collective-permute-start = (bf16[128,4,512]{2,0,1:T(8,128)(2,1)S(1)}, bf16[128,4,512]{2,0,1:T(8,128)(2,1)S(1)}, u32[]{:S(2)}, u32[]{:S(2)}) collective-permute-start(bf16[128,4,512]{2,0,1:T(8,128)(2,1)S(1)} %get-tuple-element.12), channel_id=1, source_target_pairs={{16,0},{32,16},{48,32},{64,48},{80,64},{96,80},{112,96},{17,1},{33... | collective-permute-start | bytes 1572872 | tf_op jit(solution)/shard_map/ppermute | solution.py:15
  30.4 21.4 %collective-permute-start.2 = (bf16[128,4,512]{2,0,1:T(8,128)(2,1)S(1)}, bf16[128,4,512]{2,0,1:T(8,128)(2,1)S(1)}, u32[]{:S(2)}, u32[]{:S(2)}) collective-permute-start(bf16[128,4,512]{2,0,1:T(8,128)(2,1)S(1)} %get-tuple-element.10), channel_id=1, source_target_pairs={{0,16},{16,32},{32,48},{48,64},{64,80},{80,96},{96,112},{1,17},{17... | collective-permute-start | bytes 1572872 | tf_op jit(solution)/shard_map/ppermute | solution.py:15
  73.9 92.7 %copy-start.15 = (s32[8]{0:T(128)S(1)}, s32[8]{0:T(128)}, u32[]{:S(2)}) copy-start(s32[8]{0:T(128)} %param.14) | copy-start | bytes 100
  74.0 150.0 %all-gather.2.cloned.1.call-start = ((), (), s32[]{:S(2)}) async-start(), calls=%async_computation.2 | async-start | bytes 4456448 | tf_op jit(solution)/shard_map/all_gather | solution.py:105
  232.6 1.9 copy-start.8
  258.7 0.6 copy-start.13
  261.2 0.8 copy-start.3
  294.4 0.6 copy-start.11
  295.8 2.1 copy-start.5
  297.9 1.4 copy-start.2
  323.6 27.7 %copy-start.12 = (f32[128,128]{1,0:T(8,128)}, f32[128,128]{1,0:T(8,128)S(1)}, u32[]{:S(2)}) copy-start(f32[128,128]{1,0:T(8,128)S(1)} %fusion.34) | copy-start | bytes 196612
  352.2 79.3 %copy-start.4 = (f32[896,128]{1,0:T(8,128)S(1)}, f32[896,128]{1,0:T(8,128)}, u32[]{:S(2)}) copy-start(f32[896,128]{1,0:T(8,128)} %copy-done.3) | copy-start | bytes 1376260
  353.2 1.0 copy-start.7
  354.2 78.8 %copy-start.6 = (f32[768,128]{1,0:T(8,128)S(1)}, f32[768,128]{1,0:T(8,128)}, u32[]{:S(2)}) copy-start(f32[768,128]{1,0:T(8,128)} %copy-done.5) | copy-start | bytes 1179652
  405.4 0.6 copy-start.9
  406.9 29.2 %copy-start.10 = (f32[128,128]{1,0:T(8,128)S(1)}, f32[128,128]{1,0:T(8,128)}, u32[]{:S(2)}) copy-start(f32[128,128]{1,0:T(8,128)} %copy-done.9) | copy-start | bytes 196612
Sparse Core Ops, SparseCore 0:
  74.1 90.7 reduce-scatter.1
  167.0 56.9 all-gather.1
where the time goes:
time: 478 us; the launch traced here: 469 us
  other arithmetic  208 us (44%)
  waiting for transfers between devices  144 us (30%)
  matrix products  52 us (11%)
  local copies, waits for them, and re-layouts  33.9 us (7%)
  between operations  19.6 us (4%)
  starting transfers between devices  11.8 us (2%)
    another operation x24, other arithmetic, cholesky_solve(): factor = jnp.linalg.cholesky(diag)  101 us
    reduce_scatter x1, waiting for transfers between devices, per_device(): lax.psum_scatter(jnp.einsum('prk,lpr->kl', site_tensor, block_rows, prefe...  90.8 us
    another operation x16, other arithmetic, cholesky_solve(): lax.linalg.triangular_solve(factor, eye, left_side=True, lower=True)  85.3 us
    all_gather x1, waiting for transfers between devices, per_device(): gathered = lax.all_gather(contracted, 'row', axis=0, tiled=True)  53.2 us
    dot_general x1, matrix products, per_device(): jnp.einsum('prk,lpr->kl', site_tensor, block_rows, preferred_element_type...  14.4 us
    dot_general x7, matrix products, cholesky_solve(): lax.dot_general(panel, panel, (((1,), (1,)), ((), ())), precision=HI, pre...  12.9 us
    ppermute x4, starting transfers between devices, shifted(): return lax.ppermute(x, axis, pairs)  11.8 us
  transfers between devices with their start and end apart: 6, of which 2 were waited for; matrix products, arithmetic and copies ran while one was open for 4% of the time, Pallas kernels for 0%

commit v1 on v0

--- a/solution.py
+++ b/solution.py
@@ -7,6 +7,12 @@
 KOUT = 2048
 BLOCK = 128
 HI = lax.Precision.HIGHEST
+
+
+def joined_along(parts, dim):
+    shape = list(parts.shape[1:])
+    shape[dim] *= parts.shape[0]
+    return jnp.moveaxis(parts, 0, dim).reshape(shape)
 
 
 def shifted(x, axis, by):
@@ -102,7 +108,19 @@
         scatter_dimension=0,
         tiled=True,
     ).astype(jnp.bfloat16)
-    gathered = lax.all_gather(contracted, "row", axis=0, tiled=True)
+    devices = lax.axis_size("row")
+    pairs_2 = [(i_2, (i_2 + 1) % devices) for i_2 in range(devices)]
+    back = [(b_2, a_2) for a_2, b_2 in pairs_2]
+    lower, upper = ([], [])
+    for step in range(devices - 1):
+        if step % 2 == 0:
+            lower.append(lax.ppermute(lower[-1] if lower else contracted, "row", pairs_2))
+        else:
+            upper.append(lax.ppermute(upper[-1] if upper else contracted, "row", back))
+    blocks = jnp.stack([*lower[::-1], contracted, *upper])
+    shift = lax.axis_index("row") - len(lower)
+    blocks = blocks[(jnp.arange(devices) - shift) % devices]
+    gathered = joined_along(blocks, 0)
     gram_matrix = lax.dot_general(
         gathered, gathered, (((0,), (0,)), ((), ())), preferred_element_type=jnp.float32
     )

time: 478 us -> 527 us (1.10)
  starting transfers between devices: 11.8 us -> 51.7 us
  local copies, waits for them, and re-layouts: 33.9 us -> 50.6 us
  waiting for transfers between devices: 144 us -> 131 us
    all_gather x1 -> x0, waiting for transfers between devices: 53.2 us -> none  [per_device(): gathered = lax.all_gather(contracted, 'row', axis=0, tiled=True)]
    ppermute x0 -> x15, waiting for transfers between devices: none -> 40.1 us  [the longest x8 40.1 us: per_device(): lax.ppermute(lower[-1] if lower else contracted, 'row', pairs_2)]
    ppermute x0 -> x15, starting transfers between devices: none -> 39.7 us  [the longest x7 38.2 us: per_device(): upper.append(lax.ppermute(upper[-1] if upper else contracted, 'row', back))]
    unnamed x32 -> x48, local copies, waits for them, and re-layouts: 8.85 us -> 19.6 us
  transfers between devices with their start and end apart: 6 -> 20, of which waited for: 2 -> 9; matrix products, arithmetic and copies ran while one was open for 4% -> 6% of each run, Pallas kernels for 0% -> 0%
where the time goes in v1:
time: 527 us; the launch traced here: 517 us
  other arithmetic  209 us (40%)
  waiting for transfers between devices  131 us (25%)
  matrix products  54.6 us (10%)
  starting transfers between devices  51.7 us (10%)
  local copies, waits for them, and re-layouts  50.6 us (10%)
  between operations  19.8 us (4%)
    another operation x24, other arithmetic, cholesky_solve(): factor = jnp.linalg.cholesky(diag)  101 us
    reduce_scatter x1, waiting for transfers between devices, per_device(): lax.psum_scatter(jnp.einsum('prk,lpr->kl', site_tensor, block_rows, prefe...  91 us
    another operation x16, other arithmetic, cholesky_solve(): lax.linalg.triangular_solve(factor, eye, left_side=True, lower=True)  85.8 us
    ppermute x8, waiting for transfers between devices, per_device(): lax.ppermute(lower[-1] if lower else contracted, 'row', pairs_2)  40.1 us
    ppermute x7, starting transfers between devices, per_device(): upper.append(lax.ppermute(upper[-1] if upper else contracted, 'row', back))  38.2 us
    unnamed x48, local copies, waits for them, and re-layouts  19.6 us
    dot_general x1, matrix products, per_device(): jnp.einsum('prk,lpr->kl', site_tensor, block_rows, preferred_element_type...  14.5 us
    dot_general x7, matrix products, cholesky_solve(): lax.dot_general(panel, panel, (((1,), (1,)), ((), ())), precision=HI, pre...  12.9 us
  transfers between devices with their start and end apart: 20, of which 9 were waited for; matrix products, arithmetic and copies ran while one was open for 6% of the time, Pallas kernels for 0%

profile of v1, /device:TPU:0, one launch (start us, length us, event | category | flops | bytes accessed | tf_op | source)
XLA Modules:
  0.0 516.6 jit_solution(8982979294557651609)
XLA Ops:
  11.7 5.1 copy_select_fusion
  16.8 1.9 copy-done
  20.3 3.1 collective-permute-start.3
  26.9 2.0 fusion.9
  30.1 6.3 %collective-permute-start.2 = (bf16[128,4,512]{2,0,1:T(8,128)(2,1)S(1)}, bf16[128,4,512]{2,0,1:T(8,128)(2,1)S(1)}, u32[]{:S(2)}, u32[]{:S(2)}) collective-permute-start(bf16[128,4,512]{2,0,1:T(8,128)(2,1)S(1)} %get-tuple-element.10), channel_id=1, source_target_pairs={{0,16},{16,32},{32,48},{48,64},{64,80},{80,96},{96,112},{1,17},{17... | collective-permute-start | bytes 1572872 | tf_op jit(solution)/shard_map/ppermute | solution.py:21
  36.5 2.5 concatenate.6
  40.7 5.6 %dynamic_update_slice.12 = bf16[1152,4,512]{2,0,1:T(8,128)(2,1)} dynamic-update-slice(bf16[1152,4,512]{2,0,1:T(8,128)(2,1)} %concatenate.6, bf16[128,4,512]{2,0,1:T(8,128)(2,1)S(1)} %fusion.7, s32[]{:T(128)S(6)} %select_n.82, s32[]{:T(128)} %constant.68.clone.1, s32[]{:T(128)} %constant.68.clone.1) | dynamic-update-slice | bytes 1048580 | tf_op jit(solution)/shard_map/dynamic_update_slice | solution.py:99
  46.3 5.5 %dynamic_update_slice.13 = bf16[1152,4,512]{2,0,1:T(8,128)(2,1)} dynamic-update-slice(bf16[1152,4,512]{2,0,1:T(8,128)(2,1)} %dynamic_update_slice.12, bf16[128,4,512]{2,0,1:T(8,128)(2,1)S(1)} %get-tuple-element.9, s32[]{:T(128)S(6)} %select_n.87, s32[]{:T(128)} %constant.68.clone.1, s32[]{:T(128)} %constant.68.clone.1) | dynamic-update-slice | bytes 1048580 | tf_op jit(solution)/shard_map/dynamic_update_slice | solution.py:100
  51.8 2.2 fusion.14
  54.0 5.5 %dynamic_update_slice.15 = bf16[1152,4,512]{2,0,1:T(8,128)(2,1)} dynamic-update-slice(bf16[1152,4,512]{2,0,1:T(8,128)(2,1)} %fusion.14, bf16[128,4,512]{2,0,1:T(8,128)(2,1)S(1)} %get-tuple-element.11, s32[]{:T(128)S(6)} %select_n.85, s32[]{:T(128)} %constant.68.clone.1, s32[]{:T(128)} %constant.68.clone.1) | dynamic-update-slice | bytes 1048580 | tf_op jit(solution)/shard_map/dynamic_update_slice | solution.py:102
  59.5 14.5 %fusion.2 = f32[2048,1024]{0,1:T(8,128)} fusion(bf16[1,4,512,2048]{3,2,1,0:T(8,128)(2,1)} %param.10, bf16[1152,4,512]{2,0,1:T(8,128)(2,1)} %dynamic_update_slice.15), kind=kOutput, calls=%fused_computation.3 | convolution fusion | flops 8589934592 | bytes 20971520 | tf_op jit(solution)/shard_map/prk,lpr->kl/dot_general | solution.py:106
  74.0 91.0 %reduce-scatter.2.cloned.1.call-done = f32[128,1024]{0,1:T(8,128)} async-done(((f32[2048,1024]{0,1:T(8,128)}), f32[128,1024]{0,1:T(8,128)}) %reduce-scatter.2.cloned.1.call-update) | async-done | bytes 524304 | tf_op jit(solution)/shard_map/reduce_scatter | solution.py:105
  167.7 8.7 %collective-permute-done.4 = bf16[128,1024]{0,1:T(8,128)(2,1)S(1)} collective-permute-done((bf16[128,1024]{0,1:T(8,128)(2,1)S(1)}, bf16[128,1024]{0,1:T(8,128)(2,1)S(1)}, u32[]{:S(2)}, u32[]{:S(2)}) %collective-permute-start.4) | collective-permute-done | bytes 262176 | tf_op jit(solution)/shard_map/ppermute | solution.py:117
  176.4 5.3 %collective-permute-start.12 = (bf16[128,1024]{0,1:T(8,128)(2,1)S(1)}, bf16[128,1024]{0,1:T(8,128)(2,1)S(1)}, u32[]{:S(2)}, u32[]{:S(2)}) collective-permute-start(bf16[128,1024]{0,1:T(8,128)(2,1)S(1)} %convert_element_type.87), channel_id=1, source_target_pairs={{1,0},{2,1},{3,2},{4,3},{5,4},{6,5},{7,6},{8,7},{9,8},{10,9},{11,1... | collective-permute-start | bytes 786440 | tf_op jit(solution)/shard_map/ppermute | solution.py:119
  181.8 4.3 collective-permute-done.5
  186.1 5.3 %collective-permute-start.13 = (bf16[128,1024]{0,1:T(8,128)(2,1)S(1)}, bf16[128,1024]{0,1:T(8,128)(2,1)S(1)}, u32[]{:S(2)}, u32[]{:S(2)}) collective-permute-start(bf16[128,1024]{0,1:T(8,128)(2,1)S(1)} %collective-permute-done.12), channel_id=1, source_target_pairs={{1,0},{2,1},{3,2},{4,3},{5,4},{6,5},{7,6},{8,7},{9,8},{10,9},{11,1... | collective-permute-start | bytes 786440 | tf_op jit(solution)/shard_map/ppermute | solution.py:119
  191.5 4.3 collective-permute-done.6
  195.8 5.3 %collective-permute-start.14 = (bf16[128,1024]{0,1:T(8,128)(2,1)S(1)}, bf16[128,1024]{0,1:T(8,128)(2,1)S(1)}, u32[]{:S(2)}, u32[]{:S(2)}) collective-permute-start(bf16[128,1024]{0,1:T(8,128)(2,1)S(1)} %collective-permute-done.13), channel_id=1, source_target_pairs={{1,0},{2,1},{3,2},{4,3},{5,4},{6,5},{7,6},{8,7},{9,8},{10,9},{11,1... | collective-permute-start | bytes 786440 | tf_op jit(solution)/shard_map/ppermute | solution.py:119
  201.2 4.3 collective-permute-done.7
  205.5 5.4 %collective-permute-start.15 = (bf16[128,1024]{0,1:T(8,128)(2,1)S(1)}, bf16[128,1024]{0,1:T(8,128)(2,1)S(1)}, u32[]{:S(2)}, u32[]{:S(2)}) collective-permute-start(bf16[128,1024]{0,1:T(8,128)(2,1)S(1)} %collective-permute-done.14), channel_id=1, source_target_pairs={{1,0},{2,1},{3,2},{4,3},{5,4},{6,5},{7,6},{8,7},{9,8},{10,9},{11,1... | collective-permute-start | bytes 786440 | tf_op jit(solution)/shard_map/ppermute | solution.py:119
  210.9 5.2 %collective-permute-done.8 = bf16[128,1024]{0,1:T(8,128)(2,1)S(1)} collective-permute-done((bf16[128,1024]{0,1:T(8,128)(2,1)S(1)}, bf16[128,1024]{0,1:T(8,128)(2,1)S(1)}, u32[]{:S(2)}, u32[]{:S(2)}) %collective-permute-start.8) | collective-permute-done | bytes 262176 | tf_op jit(solution)/shard_map/ppermute | solution.py:117
  216.1 5.9 %collective-permute-start.16 = (bf16[128,1024]{0,1:T(8,128)(2,1)S(1)}, bf16[128,1024]{0,1:T(8,128)(2,1)S(1)}, u32[]{:S(2)}, u32[]{:S(2)}) collective-permute-start(bf16[128,1024]{0,1:T(8,128)(2,1)S(1)} %collective-permute-done.15), channel_id=1, source_target_pairs={{1,0},{2,1},{3,2},{4,3},{5,4},{6,5},{7,6},{8,7},{9,8},{10,9},{11,1... | collective-permute-start | bytes 786440 | tf_op jit(solution)/shard_map/ppermute | solution.py:119
  222.0 5.9 %collective-permute-done.9 = bf16[128,1024]{0,1:T(8,128)(2,1)S(1)} collective-permute-done((bf16[128,1024]{0,1:T(8,128)(2,1)S(1)}, bf16[128,1024]{0,1:T(8,128)(2,1)S(1)}, u32[]{:S(2)}, u32[]{:S(2)}) %collective-permute-start.9) | collective-permute-done | bytes 262176 | tf_op jit(solution)/shard_map/ppermute | solution.py:117
  230.5 5.4 %collective-permute-start.17 = (bf16[128,1024]{0,1:T(8,128)(2,1)S(1)}, bf16[128,1024]{0,1:T(8,128)(2,1)S(1)}, u32[]{:S(2)}, u32[]{:S(2)}) collective-permute-start(bf16[128,1024]{0,1:T(8,128)(2,1)S(1)} %collective-permute-done.16), channel_id=1, source_target_pairs={{1,0},{2,1},{3,2},{4,3},{5,4},{6,5},{7,6},{8,7},{9,8},{10,9},{11,1... | collective-permute-start | bytes 786440 | tf_op jit(solution)/shard_map/ppermute | solution.py:119
  235.9 4.5 collective-permute-done.10
  242.1 5.4 %collective-permute-start.18 = (bf16[128,1024]{0,1:T(8,128)(2,1)S(1)}, bf16[128,1024]{0,1:T(8,128)(2,1)S(1)}, u32[]{:S(2)}, u32[]{:S(2)}) collective-permute-start(bf16[128,1024]{0,1:T(8,128)(2,1)S(1)} %collective-permute-done.17), channel_id=1, source_target_pairs={{1,0},{2,1},{3,2},{4,3},{5,4},{6,5},{7,6},{8,7},{9,8},{10,9},{11,1... | collective-permute-start | bytes 786440 | tf_op jit(solution)/shard_map/ppermute | solution.py:119
  247.5 2.8 collective-permute-done.11
  263.8 5.2 %gather_fusion = bf16[16,128,1024]{1,2,0:T(8,128)(2,1)} fusion(bf16[16,128,1024]{1,2,0:T(8,128)(2,1)} %bitcast_dynamic-update-slice_fusion, s32[1024]{0:T(1024)S(1)} %pad_clamp_fusion), kind=kCustom, calls=%fused_computation | custom fusion | bytes 8388672 | tf_op jit(solution)/shard_map/gather | solution.py:122
  269.0 7.8 %bitcast_add_fusion = f32[1024,1024]{0,1:T(8,128)S(1)} fusion(bf16[16,128,1024]{1,2,0:T(8,128)(2,1)} %gather_fusion, f32[1024]{0:T(1024)S(1)} %fusion.84), kind=kOutput, calls=%fused_computation.5 | convolution fusion | flops 4298113024 | bytes 8392704 | tf_op jit(solution)/shard_map/dot_general | solution.py:124
  279.7 11.7 %cholesky.134 = f32[128,128]{1,0:T(8,128)S(1)} custom-call(f32[128,128]{1,0:T(8,128)S(1)} %fusion.81), custom_call_target="Cholesky" | custom-call | tf_op jit(solution)/shard_map/jit(cholesky)/cholesky | solution.py:49
  292.7 9.8 %custom-call.12 = f32[1,128,128]{1,2,0:T(8,128)S(1)} custom-call(f32[1,128,128]{2,1,0:T(8,128)S(1)} %fusion.44), custom_call_target="InvertDiagBlocksLowerTriangular" | custom-call | tf_op jit(solution)/shard_map/triangular_solve/custom-call.0 | solution.py:50
  306.1 4.6 slice_subtract_fusion
  312.9 12.7 %cholesky.145 = f32[128,128]{1,0:T(8,128)S(1)} custom-call(f32[128,128]{1,0:T(8,128)} %fusion.79), custom_call_target="Cholesky" | custom-call | tf_op jit(solution)/shard_map/jit(cholesky)/cholesky | solution.py:49
  327.5 11.3 %custom-call.13 = f32[1,128,128]{1,2,0:T(8,128)} custom-call(f32[1,128,128]{2,1,0:T(8,128)} %fusion.45), custom_call_target="InvertDiagBlocksLowerTriangular" | custom-call | tf_op jit(solution)/shard_map/triangular_solve/custom-call.0 | solution.py:50
  340.7 2.0 slice_subtract_fusion.1
  345.2 11.7 %cholesky.156 = f32[128,128]{1,0:T(8,128)S(1)} custom-call(f32[128,128]{1,0:T(8,128)S(1)} %fusion.77), custom_call_target="Cholesky" | custom-call | tf_op jit(solution)/shard_map/jit(cholesky)/cholesky | solution.py:49
  358.3 10.2 %custom-call.14 = f32[1,128,128]{1,2,0:T(8,128)S(1)} custom-call(f32[1,128,128]{2,1,0:T(8,128)S(1)} %fusion.46), custom_call_target="InvertDiagBlocksLowerTriangular" | custom-call | tf_op jit(solution)/shard_map/triangular_solve/custom-call.0 | solution.py:50
  370.5 2.9 slice_subtract_fusion.2
  373.5 11.7 %cholesky.167 = f32[128,128]{1,0:T(8,128)S(1)} custom-call(f32[128,128]{1,0:T(8,128)S(1)} %fusion.75), custom_call_target="Cholesky" | custom-call | tf_op jit(solution)/shard_map/jit(cholesky)/cholesky | solution.py:49
  386.5 9.8 %custom-call.15 = f32[1,128,128]{1,2,0:T(8,128)S(1)} custom-call(f32[1,128,128]{2,1,0:T(8,128)S(1)} %fusion.47), custom_call_target="InvertDiagBlocksLowerTriangular" | custom-call | tf_op jit(solution)/shard_map/triangular_solve/custom-call.0 | solution.py:50
  400.2 11.9 %cholesky.178 = f32[128,128]{1,0:T(8,128)S(1)} custom-call(f32[128,128]{1,0:T(8,128)S(1)} %fusion.73), custom_call_target="Cholesky" | custom-call | tf_op jit(solution)/shard_map/jit(cholesky)/cholesky | solution.py:49
  413.4 9.8 %custom-call.16 = f32[1,128,128]{1,2,0:T(8,128)S(1)} custom-call(f32[1,128,128]{2,1,0:T(8,128)S(1)} %fusion.48), custom_call_target="InvertDiagBlocksLowerTriangular" | custom-call | tf_op jit(solution)/shard_map/triangular_solve/custom-call.0 | solution.py:50
  426.8 11.7 %cholesky.189 = f32[128,128]{1,0:T(8,128)S(1)} custom-call(f32[128,128]{1,0:T(8,128)S(1)} %fusion.71), custom_call_target="Cholesky" | custom-call | tf_op jit(solution)/shard_map/jit(cholesky)/cholesky | solution.py:49
  439.7 9.8 %custom-call.17 = f32[1,128,128]{1,2,0:T(8,128)S(1)} custom-call(f32[1,128,128]{2,1,0:T(8,128)S(1)} %fusion.49), custom_call_target="InvertDiagBlocksLowerTriangular" | custom-call | tf_op jit(solution)/shard_map/triangular_solve/custom-call.0 | solution.py:50
  450.9 11.7 %cholesky.200 = f32[128,128]{1,0:T(8,128)S(1)} custom-call(f32[128,128]{1,0:T(8,128)S(1)} %fusion.69), custom_call_target="Cholesky" | custom-call | tf_op jit(solution)/shard_map/jit(cholesky)/cholesky | solution.py:49
  463.9 9.8 %custom-call.18 = f32[1,128,128]{1,2,0:T(8,128)S(1)} custom-call(f32[1,128,128]{2,1,0:T(8,128)S(1)} %fusion.50), custom_call_target="InvertDiagBlocksLowerTriangular" | custom-call | tf_op jit(solution)/shard_map/triangular_solve/custom-call.0 | solution.py:50
  483.0 12.0 %cholesky.211 = f32[128,128]{1,0:T(8,128)S(1)} custom-call(f32[128,128]{1,0:T(8,128)S(1)} %fusion.67), custom_call_target="Cholesky" | custom-call | tf_op jit(solution)/shard_map/jit(cholesky)/cholesky | solution.py:49
  496.3 9.8 %custom-call.19 = f32[1,128,128]{1,2,0:T(8,128)S(1)} custom-call(f32[1,128,128]{2,1,0:T(8,128)S(1)} %fusion.51), custom_call_target="InvertDiagBlocksLowerTriangular" | custom-call | tf_op jit(solution)/shard_map/triangular_solve/custom-call.0 | solution.py:50
  (174 shorter events, 75.4 us)
Async XLA Ops:
  6.5 158.5 %reduce-scatter.2.cloned.1.call-start = ((), (), s32[]{:S(2)}) async-start(), calls=%async_computation.1 | async-start | bytes 8912896 | tf_op jit(solution)/shard_map/reduce_scatter | solution.py:105
  16.8 1.9 copy-start
  18.8 8.0 %copy-start.15 = (f32[2,8,128]{2,1,0:T(8,128)S(1)}, f32[2,8,128]{2,1,0:T(8,128)}, u32[]{:S(2)}) copy-start(f32[2,8,128]{2,1,0:T(8,128)} %param.13) | copy-start | bytes 24580
  19.0 7.9 %collective-permute-start.1 = (bf16[128,4,512]{2,0,1:T(8,128)(2,1)S(1)}, bf16[128,4,512]{2,0,1:T(8,128)(2,1)S(1)}, u32[]{:S(2)}, u32[]{:S(2)}) collective-permute-start(bf16[128,4,512]{2,0,1:T(8,128)(2,1)S(1)} %get-tuple-element.13), channel_id=1, source_target_pairs={{16,0},{32,16},{48,32},{64,48},{80,64},{96,80},{112,96},{17,1},{33... | collective-permute-start | bytes 1572872 | tf_op jit(solution)/shard_map/ppermute | solution.py:21
  20.3 6.6 %collective-permute-start.3 = (bf16[128,4,512]{2,0,1:T(8,128)(2,1)S(1)}, bf16[128,4,512]{2,0,1:T(8,128)(2,1)S(1)}, u32[]{:S(2)}, u32[]{:S(2)}) collective-permute-start(bf16[128,4,512]{2,0,1:T(8,128)(2,1)S(1)} %get-tuple-element.14), channel_id=1, source_target_pairs={{0,16},{16,32},{32,48},{48,64},{64,80},{80,96},{96,112},{1,17},{17... | collective-permute-start | bytes 1572872 | tf_op jit(solution)/shard_map/ppermute | solution.py:21
  25.3 11.2 %copy-start.1 = (bf16[1024,4,512]{2,0,1:T(8,128)(2,1)S(1)}, bf16[1024,4,512]{2,0,1:T(8,128)(2,1)}, u32[]{:S(2)}) copy-start(bf16[1024,4,512]{2,0,1:T(8,128)(2,1)} %copy-done) | copy-start | bytes 12582916
  28.8 11.5 %collective-permute-start = (bf16[128,4,512]{2,0,1:T(8,128)(2,1)S(1)}, bf16[128,4,512]{2,0,1:T(8,128)(2,1)S(1)}, u32[]{:S(2)}, u32[]{:S(2)}) collective-permute-start(bf16[128,4,512]{2,0,1:T(8,128)(2,1)S(1)} %get-tuple-element.12), channel_id=1, source_target_pairs={{16,0},{32,16},{48,32},{64,48},{80,64},{96,80},{112,96},{17,1},{33... | collective-permute-start | bytes 1572872 | tf_op jit(solution)/shard_map/ppermute | solution.py:21
  30.1 21.7 %collective-permute-start.2 = (bf16[128,4,512]{2,0,1:T(8,128)(2,1)S(1)}, bf16[128,4,512]{2,0,1:T(8,128)(2,1)S(1)}, u32[]{:S(2)}, u32[]{:S(2)}) collective-permute-start(bf16[128,4,512]{2,0,1:T(8,128)(2,1)S(1)} %get-tuple-element.10), channel_id=1, source_target_pairs={{0,16},{16,32},{32,48},{48,64},{64,80},{80,96},{96,112},{1,17},{17... | collective-permute-start | bytes 1572872 | tf_op jit(solution)/shard_map/ppermute | solution.py:21
  74.0 153.9 %copy-start.16 = (s32[8]{0:T(128)S(1)}, s32[8]{0:T(128)}, u32[]{:S(2)}) copy-start(s32[8]{0:T(128)} %param.14) | copy-start | bytes 100
  165.1 92.9 %copy-start.7 = (f32[128,1024]{0,1:T(8,128)S(1)}, f32[128,1024]{0,1:T(8,128)}, u32[]{:S(2)}) copy-start(f32[128,1024]{0,1:T(8,128)} %reduce-scatter.2.cloned.1.call-done) | copy-start | bytes 1572868
  166.2 10.2 %collective-permute-start.4 = (bf16[128,1024]{0,1:T(8,128)(2,1)S(1)}, bf16[128,1024]{0,1:T(8,128)(2,1)S(1)}, u32[]{:S(2)}, u32[]{:S(2)}) collective-permute-start(bf16[128,1024]{0,1:T(8,128)(2,1)S(1)} %convert_element_type.87), channel_id=1, source_target_pairs={{0,1},{1,2},{2,3},{3,4},{4,5},{5,6},{6,7},{7,8},{8,9},{9,10},{10,1... | collective-permute-start | bytes 786440 | tf_op jit(solution)/shard_map/ppermute | solution.py:117
  176.4 9.7 %collective-permute-start.5 = (bf16[128,1024]{0,1:T(8,128)(2,1)S(1)}, bf16[128,1024]{0,1:T(8,128)(2,1)S(1)}, u32[]{:S(2)}, u32[]{:S(2)}) collective-permute-start(bf16[128,1024]{0,1:T(8,128)(2,1)S(1)} %collective-permute-done.4), channel_id=1, source_target_pairs={{0,1},{1,2},{2,3},{3,4},{4,5},{5,6},{6,7},{7,8},{8,9},{9,10},{10,1... | collective-permute-start | bytes 786440 | tf_op jit(solution)/shard_map/ppermute | solution.py:117
  176.4 9.7 %collective-permute-start.12 = (bf16[128,1024]{0,1:T(8,128)(2,1)S(1)}, bf16[128,1024]{0,1:T(8,128)(2,1)S(1)}, u32[]{:S(2)}, u32[]{:S(2)}) collective-permute-start(bf16[128,1024]{0,1:T(8,128)(2,1)S(1)} %convert_element_type.87), channel_id=1, source_target_pairs={{1,0},{2,1},{3,2},{4,3},{5,4},{6,5},{7,6},{8,7},{9,8},{10,9},{11,1... | collective-permute-start | bytes 786440 | tf_op jit(solution)/shard_map/ppermute | solution.py:119
  186.1 9.7 %collective-permute-start.6 = (bf16[128,1024]{0,1:T(8,128)(2,1)S(1)}, bf16[128,1024]{0,1:T(8,128)(2,1)S(1)}, u32[]{:S(2)}, u32[]{:S(2)}) collective-permute-start(bf16[128,1024]{0,1:T(8,128)(2,1)S(1)} %collective-permute-done.5), channel_id=1, source_target_pairs={{0,1},{1,2},{2,3},{3,4},{4,5},{5,6},{6,7},{7,8},{8,9},{9,10},{10,1... | collective-permute-start | bytes 786440 | tf_op jit(solution)/shard_map/ppermute | solution.py:117
  186.1 9.7 %collective-permute-start.13 = (bf16[128,1024]{0,1:T(8,128)(2,1)S(1)}, bf16[128,1024]{0,1:T(8,128)(2,1)S(1)}, u32[]{:S(2)}, u32[]{:S(2)}) collective-permute-start(bf16[128,1024]{0,1:T(8,128)(2,1)S(1)} %collective-permute-done.12), channel_id=1, source_target_pairs={{1,0},{2,1},{3,2},{4,3},{5,4},{6,5},{7,6},{8,7},{9,8},{10,9},{11,1... | collective-permute-start | bytes 786440 | tf_op jit(solution)/shard_map/ppermute | solution.py:119
  195.8 9.7 %collective-permute-start.7 = (bf16[128,1024]{0,1:T(8,128)(2,1)S(1)}, bf16[128,1024]{0,1:T(8,128)(2,1)S(1)}, u32[]{:S(2)}, u32[]{:S(2)}) collective-permute-start(bf16[128,1024]{0,1:T(8,128)(2,1)S(1)} %collective-permute-done.6), channel_id=1, source_target_pairs={{0,1},{1,2},{2,3},{3,4},{4,5},{5,6},{6,7},{7,8},{8,9},{9,10},{10,1... | collective-permute-start | bytes 786440 | tf_op jit(solution)/shard_map/ppermute | solution.py:117
  195.8 9.7 %collective-permute-start.14 = (bf16[128,1024]{0,1:T(8,128)(2,1)S(1)}, bf16[128,1024]{0,1:T(8,128)(2,1)S(1)}, u32[]{:S(2)}, u32[]{:S(2)}) collective-permute-start(bf16[128,1024]{0,1:T(8,128)(2,1)S(1)} %collective-permute-done.13), channel_id=1, source_target_pairs={{1,0},{2,1},{3,2},{4,3},{5,4},{6,5},{7,6},{8,7},{9,8},{10,9},{11,1... | collective-permute-start | bytes 786440 | tf_op jit(solution)/shard_map/ppermute | solution.py:119
  205.5 10.6 %collective-permute-start.8 = (bf16[128,1024]{0,1:T(8,128)(2,1)S(1)}, bf16[128,1024]{0,1:T(8,128)(2,1)S(1)}, u32[]{:S(2)}, u32[]{:S(2)}) collective-permute-start(bf16[128,1024]{0,1:T(8,128)(2,1)S(1)} %collective-permute-done.7), channel_id=1, source_target_pairs={{0,1},{1,2},{2,3},{3,4},{4,5},{5,6},{6,7},{7,8},{8,9},{9,10},{10,1... | collective-permute-start | bytes 786440 | tf_op jit(solution)/shard_map/ppermute | solution.py:117
  205.5 10.6 %collective-permute-start.15 = (bf16[128,1024]{0,1:T(8,128)(2,1)S(1)}, bf16[128,1024]{0,1:T(8,128)(2,1)S(1)}, u32[]{:S(2)}, u32[]{:S(2)}) collective-permute-start(bf16[128,1024]{0,1:T(8,128)(2,1)S(1)} %collective-permute-done.14), channel_id=1, source_target_pairs={{1,0},{2,1},{3,2},{4,3},{5,4},{6,5},{7,6},{8,7},{9,8},{10,9},{11,1... | collective-permute-start | bytes 786440 | tf_op jit(solution)/shard_map/ppermute | solution.py:119
  216.1 11.8 %collective-permute-start.9 = (bf16[128,1024]{0,1:T(8,128)(2,1)S(1)}, bf16[128,1024]{0,1:T(8,128)(2,1)S(1)}, u32[]{:S(2)}, u32[]{:S(2)}) collective-permute-start(bf16[128,1024]{0,1:T(8,128)(2,1)S(1)} %collective-permute-done.8), channel_id=1, source_target_pairs={{0,1},{1,2},{2,3},{3,4},{4,5},{5,6},{6,7},{7,8},{8,9},{9,10},{10,1... | collective-permute-start | bytes 786440 | tf_op jit(solution)/shard_map/ppermute | solution.py:117
  216.1 14.3 %collective-permute-start.16 = (bf16[128,1024]{0,1:T(8,128)(2,1)S(1)}, bf16[128,1024]{0,1:T(8,128)(2,1)S(1)}, u32[]{:S(2)}, u32[]{:S(2)}) collective-permute-start(bf16[128,1024]{0,1:T(8,128)(2,1)S(1)} %collective-permute-done.15), channel_id=1, source_target_pairs={{1,0},{2,1},{3,2},{4,3},{5,4},{6,5},{7,6},{8,7},{9,8},{10,9},{11,1... | collective-permute-start | bytes 786440 | tf_op jit(solution)/shard_map/ppermute | solution.py:119
  227.9 12.5 %copy-start.14 = (bf16[128,1024]{0,1:T(8,128)(2,1)}, bf16[128,1024]{0,1:T(8,128)(2,1)S(1)}, u32[]{:S(2)}) copy-start(bf16[128,1024]{0,1:T(8,128)(2,1)S(1)} %collective-permute-done.9) | copy-start | bytes 786436
  227.9 12.5 %collective-permute-start.10 = (bf16[128,1024]{0,1:T(8,128)(2,1)S(1)}, bf16[128,1024]{0,1:T(8,128)(2,1)}, u32[]{:S(2)}, u32[]{:S(2)}) collective-permute-start(bf16[128,1024]{0,1:T(8,128)(2,1)S(1)} %collective-permute-done.9), channel_id=1, source_target_pairs={{0,1},{1,2},{2,3},{3,4},{4,5},{5,6},{6,7},{7,8},{8,9},{9,10},{10,1... | collective-permute-start | bytes 786440 | tf_op jit(solution)/shard_map/ppermute | solution.py:117
  230.5 11.6 %collective-permute-start.17 = (bf16[128,1024]{0,1:T(8,128)(2,1)S(1)}, bf16[128,1024]{0,1:T(8,128)(2,1)S(1)}, u32[]{:S(2)}, u32[]{:S(2)}) collective-permute-start(bf16[128,1024]{0,1:T(8,128)(2,1)S(1)} %collective-permute-done.16), channel_id=1, source_target_pairs={{1,0},{2,1},{3,2},{4,3},{5,4},{6,5},{7,6},{8,7},{9,8},{10,9},{11,1... | collective-permute-start | bytes 786440 | tf_op jit(solution)/shard_map/ppermute | solution.py:119
  240.4 9.9 %collective-permute-start.11 = (bf16[128,1024]{0,1:T(8,128)(2,1)}, bf16[128,1024]{0,1:T(8,128)(2,1)S(1)}, u32[]{:S(2)}, u32[]{:S(2)}) collective-permute-start(bf16[128,1024]{0,1:T(8,128)(2,1)} %collective-permute-done.10), channel_id=1, source_target_pairs={{0,1},{1,2},{2,3},{3,4},{4,5},{5,6},{6,7},{7,8},{8,9},{9,10},{10,1... | collective-permute-start | bytes 786440 | tf_op jit(solution)/shard_map/ppermute | solution.py:117
  242.1 20.9 %collective-permute-start.18 = (bf16[128,1024]{0,1:T(8,128)(2,1)S(1)}, bf16[128,1024]{0,1:T(8,128)(2,1)S(1)}, u32[]{:S(2)}, u32[]{:S(2)}) collective-permute-start(bf16[128,1024]{0,1:T(8,128)(2,1)S(1)} %collective-permute-done.17), channel_id=1, source_target_pairs={{1,0},{2,1},{3,2},{4,3},{5,4},{6,5},{7,6},{8,7},{9,8},{10,9},{11,1... | collective-permute-start | bytes 786440 | tf_op jit(solution)/shard_map/ppermute | solution.py:119
  276.8 1.9 copy-start.9
  302.8 0.6 copy-start.12
  305.4 0.8 copy-start.3
  340.7 2.1 copy-start.5
  342.8 1.4 copy-start.2
  368.8 28.4 %copy-start.10 = (f32[128,128]{1,0:T(8,128)}, f32[128,128]{1,0:T(8,128)S(1)}, u32[]{:S(2)}) copy-start(f32[128,128]{1,0:T(8,128)S(1)} %fusion.34) | copy-start | bytes 196612
  397.2 77.9 %copy-start.4 = (f32[896,128]{1,0:T(8,128)S(1)}, f32[896,128]{1,0:T(8,128)}, u32[]{:S(2)}) copy-start(f32[896,128]{1,0:T(8,128)} %copy-done.3) | copy-start | bytes 1376260
  398.2 1.0 copy-start.8
  399.2 75.1 %copy-start.13 = (f32[128,128]{1,0:T(8,128)S(1)}, f32[128,128]{1,0:T(8,128)}, u32[]{:S(2)}) copy-start(f32[128,128]{1,0:T(8,128)} %copy-done.12) | copy-start | bytes 196612
  399.2 77.2 %copy-start.6 = (f32[768,128]{1,0:T(8,128)S(1)}, f32[768,128]{1,0:T(8,128)}, u32[]{:S(2)}) copy-start(f32[768,128]{1,0:T(8,128)} %copy-done.5) | copy-start | bytes 1179652
  399.3 77.6 %copy-start.11 = (f32[128,128]{1,0:T(8,128)S(1)}, f32[128,128]{1,0:T(8,128)}, u32[]{:S(2)}) copy-start(f32[128,128]{1,0:T(8,128)} %copy-done.10) | copy-start | bytes 196612
Sparse Core Ops, SparseCore 0:
  74.1 90.8 reduce-scatter.1
